TPU v7x, 32 devices: a whole 2x2x4 slice. The times are simulated.
32 devices in a mesh: tm: 8 (over z, core), space: 4 (over y, x).
Axes of the slice: x: 2, y: 2, z: 4, core: 2. Of those that a mesh axis runs over, the one named last changes fastest.
Arguments:
- volumes: float32 [8, 64, 512, 128], P('tm', 'space'), may hold values from -12 to 12
Outputs:
- corrected: float32 [8, 64, 512, 128], P('tm', 'space')
- shifts: float32 [8, 3], P('tm')
All inputs are finite; a program needn't handle non-finite values.
Results may differ from a plain program's by a relative error of at most 0.0003.
Values sent between devices are 32-bit elements; how exact they have to be, the bound alone decides.
No kernel may reach another device: no remote copies, remote signals or barrier semaphores. Data moves between devices by JAX's collectives and lax.ppermute only.
A program may use at most 128 MiB of HBM per device.

v0:
```python
import math
import jax
import jax.numpy as jnp
from jax import lax
from jax.sharding import PartitionSpec as P

X = 512
Y = 128
Z = 64
ITERS = 2
precise = lax.Precision.HIGHEST
sharpness = 256.0
floor_share = 0.05


def dft_tables(length):
    indices = jnp.arange(length, dtype=jnp.int32)
    products = indices[:, None] * indices[None, :] % length
    angles = products.astype(jnp.float32) * (2.0 * math.pi / length)
    return (jnp.cos(angles), jnp.sin(angles))


def signed_freq(indices, length):
    wrapped = jnp.where(indices < length // 2, indices, indices - length)
    return jnp.where(indices == length // 2, 0, wrapped).astype(jnp.float32)


def centred(indices, length):
    return ((indices + length // 2) % length - length // 2).astype(jnp.float32)


def mix_z(table, data):
    return jnp.einsum("kz,vz...->vk...", table, data, precision=precise)


def mix_x(table, data):
    return jnp.einsum("kx,vzx...->vzk...", table, data, precision=precise)


def mix_y(data, table):
    return jnp.dot(data, table, precision=precise)


def forward(volume, tables):
    cos_x, sin_x, cos_y, sin_y, cos_z, sin_z = tables
    real_x = mix_x(cos_x, volume)
    imag_x = -mix_x(sin_x, volume)
    real_y = mix_y(real_x, cos_y) + mix_y(imag_x, sin_y)
    imag_y = mix_y(imag_x, cos_y) - mix_y(real_x, sin_y)
    real_p, imag_p = (
        lax.all_to_all(real_y, "space", split_axis=2, concat_axis=1, tiled=True),
        lax.all_to_all(imag_y, "space", split_axis=2, concat_axis=1, tiled=True),
    )
    real_z = mix_z(cos_z, real_p) + mix_z(sin_z, imag_p)
    imag_z = mix_z(cos_z, imag_p) - mix_z(sin_z, real_p)
    return (real_z, imag_z)


def inverse(spectrum, tables):
    cos_x, sin_x, cos_y, sin_y, cos_z, sin_z = tables
    norming = 1.0 / (X * Y * Z)
    real_in, imag_in = spectrum
    real_z = mix_z(cos_z, real_in) - mix_z(sin_z, imag_in)
    imag_z = mix_z(sin_z, real_in) + mix_z(cos_z, imag_in)
    real_y = mix_y(real_z, cos_y) - mix_y(imag_z, sin_y)
    imag_y = mix_y(real_z, sin_y) + mix_y(imag_z, cos_y)
    real_s, imag_s = (
        lax.all_to_all(real_y, "space", split_axis=1, concat_axis=2, tiled=True),
        lax.all_to_all(imag_y, "space", split_axis=1, concat_axis=2, tiled=True),
    )
    return (mix_x(cos_x, real_s) - mix_x(sin_x, imag_s)) * norming


def split_pairs(spectrum):
    return [(spectrum[0], spectrum[1])]


def join_pairs(pairs):
    return (pairs[0][0], pairs[0][1])


def y_frequencies():
    return [signed_freq(jnp.arange(Y, dtype=jnp.int32), Y)]


def template_sum(spectrum):
    return lax.psum((jnp.sum(spectrum[0], axis=0), jnp.sum(spectrum[1], axis=0)), "tm")


def weight_moments(weights, coords):
    coord_z, coord_x, coord_y = coords
    weight_sum = jnp.sum(weights, axis=(1, 2, 3))
    moment_z = jnp.sum(jnp.sum(weights, axis=(2, 3)) * coord_z[None, :], axis=1)
    moment_x = jnp.sum(jnp.sum(weights, axis=(1, 3)) * coord_x[None, :], axis=1)
    moment_y = jnp.sum(jnp.sum(weights, axis=(1, 2)) * coord_y[None, :], axis=1)
    return (weight_sum, jnp.stack([moment_z, moment_x, moment_y], axis=1))


def centroid(scores, coords):
    local_top = jnp.max(scores, axis=(1, 2, 3))
    top_score = lax.pmax(local_top, "space")
    weights = jnp.exp(scores - top_score[:, None, None, None])
    weight_sum, moments = weight_moments(weights, coords)
    weight_sum, moments = lax.psum((weight_sum, moments), "space")
    return moments / weight_sum[:, None]


def apply_ramp(real_in, imag_in, shifts, freq_z, freq_x, freq_y):
    phases = (
        2.0
        * math.pi
        * (
            freq_z[None, :, None] * (shifts[:, 0] / Z)[:, None, None]
            + freq_x[None, None, :] * (shifts[:, 1] / X)[:, None, None]
        )
    )
    phases = (
        phases[..., None]
        + 2.0 * math.pi * freq_y[None, None, None, :] * (shifts[:, 2] / Y)[:, None, None, None]
    )
    cosine = jnp.cos(phases)
    sine = jnp.sin(phases)
    return (real_in * cosine - imag_in * sine, real_in * sine + imag_in * cosine)


def whiten(spec_re, spec_im, tmpl_re, tmpl_im):
    prod_re = spec_re * tmpl_re + spec_im * tmpl_im
    prod_im = spec_im * tmpl_re - spec_re * tmpl_im
    divisor = jnp.maximum(
        jnp.sqrt(prod_re * prod_re + prod_im * prod_im), floor_share * (X * Y * Z)
    )
    return (prod_re / divisor, prod_im / divisor)


def body(volumes):
    position = lax.axis_index("space")
    slab_depth = volumes.shape[1]
    pencil = X // lax.axis_size("space")
    frames = volumes.shape[0] * lax.axis_size("tm")
    tables = dft_tables(X) + dft_tables(Y) + dft_tables(Z)
    z_index = position * slab_depth + jnp.arange(slab_depth, dtype=jnp.int32)
    x_index = position * pencil + jnp.arange(pencil, dtype=jnp.int32)
    coords = (
        centred(z_index, Z),
        centred(jnp.arange(X, dtype=jnp.int32), X),
        centred(jnp.arange(Y, dtype=jnp.int32), Y),
    )
    freq_z = signed_freq(jnp.arange(Z, dtype=jnp.int32), Z)
    freq_x = signed_freq(x_index, X)
    freq_ys = y_frequencies()
    spectrum = forward(volumes, tables)
    spec_pairs = split_pairs(spectrum)
    shifted = spectrum
    for iteration in range(ITERS):
        summed = template_sum(shifted)
        template = tuple((part[None] / frames for part in summed))
        tmpl_pairs = split_pairs(template)
        white_pairs = [
            whiten(spec_pairs[0][0], spec_pairs[0][1], tmpl_pairs[0][0], tmpl_pairs[0][1])
        ]
        correlation = inverse(join_pairs(white_pairs), tables)
        shifts = centroid(sharpness * correlation, coords)
        ramped = [
            apply_ramp(spec_pairs[0][0], spec_pairs[0][1], shifts, freq_z, freq_x, freq_ys[0])
        ]
        shifted = join_pairs(ramped)
    corrected = inverse(shifted, tables)
    return (corrected, shifts)


def solution(mesh):
    in_specs = (P("tm", "space", None, None),)
    out_specs = (P("tm", "space", None, None), P("tm", None))
    return jax.shard_map(body, mesh=mesh, in_specs=in_specs, out_specs=out_specs, check_vma=False)
```

profile of v0, /device:TPU:0, one launch (start us, length us, event | category | flops | bytes accessed | tf_op | source)
XLA Modules:
  0.0 1235.6 jit_solution(4220639546576311592)
XLA Ops:
  7.2 13.2 %fusion.46 = f32[512,16,128]{2,0,1:T(8,128)S(1)} fusion(f32[1,16,512,128]{3,2,1,0:T(8,128)} %param.1), kind=kOutput, calls=%fused_computation.58 | convolution fusion | flops 6446120960 | bytes 8388608 | tf_op jit(solution)/shard_map/kx,vzx...->vzk.../dot_general | solution.py:37
  20.4 11.1 fusion.44
  63.7 34.3 %all-to-all-done = f32[1,16,512,128]{3,1,0,2:T(8,128)} async-done(((f32[1,16,512,128]{3,1,0,2:T(8,128)}), f32[1,16,512,128]{3,1,0,2:T(8,128)}, u32[]{:S(2)}, u32[]{:S(2)}) %all-to-all-start) | async-done | bytes 4194336 | tf_op jit(solution)/shard_map/all_to_all | solution.py:51
  113.4 36.6 %all-to-all-done.1 = f32[1,16,512,128]{3,1,0,2:T(8,128)} async-done(((f32[1,16,512,128]{3,1,0,2:T(8,128)}), f32[1,16,512,128]{3,1,0,2:T(8,128)}, u32[]{:S(2)}, u32[]{:S(2)}) %all-to-all-start.1) | async-done | bytes 4194336 | tf_op jit(solution)/shard_map/all_to_all | solution.py:52
  168.3 176.1 %all-reduce.9.cloned.1.call-done = (f32[64,128,128]{2,0,1:T(8,128)}, f32[64,128,128]{2,0,1:T(8,128)}) async-done(((f32[64,128,128]{2,0,1:T(8,128)}, f32[64,128,128]{2,0,1:T(8,128)}), (f32[64,128,128]{2,0,1:T(8,128)}, f32[64,128,128]{2,0,1:T(8,128)})) %all-reduce.9.cloned.1.call-update) | async-done | bytes 8388624 | tf_op jit(solution)/shard_map/psum | solution.py:87
  344.4 10.4 fusion.34
  354.8 8.4 fusion.28
  363.2 6.3 fusion.26
  369.6 6.2 subtract_bitcast_fusion.5
  375.8 6.4 add_bitcast_fusion.5
  382.2 7.1 fusion.68
  389.3 8.2 add_bitcast_fusion.4
  402.8 8.8 fusion.70
  411.6 8.2 subtract_bitcast_fusion.4
  419.8 30.4 %all-to-all-done.3 = f32[1,64,128,128]{3,2,0,1:T(8,128)} async-done(((f32[1,64,128,128]{3,2,0,1:T(8,128)}), f32[1,64,128,128]{3,2,0,1:T(8,128)}, u32[]{:S(2)}, u32[]{:S(2)}) %all-to-all-start.3) | async-done | bytes 4194336 | tf_op jit(solution)/shard_map/all_to_all | solution.py:69
  465.8 36.2 %all-to-all-done.2 = f32[1,64,128,128]{3,2,0,1:T(8,128)} async-done(((f32[1,64,128,128]{3,2,0,1:T(8,128)}), f32[1,64,128,128]{3,2,0,1:T(8,128)}, u32[]{:S(2)}, u32[]{:S(2)}) %all-to-all-start.2) | async-done | bytes 4194336 | tf_op jit(solution)/shard_map/all_to_all | solution.py:68
  512.9 12.9 %fusion.121 = f32[16,128,512]{2,1,0:T(8,128)S(1)} fusion(f32[16,512,128]{1,2,0:T(8,128)} %reshape.463), kind=kOutput, calls=%fused_computation.135 | convolution fusion | flops 6446120960 | bytes 8388608 | tf_op jit(solution)/shard_map/kx,vzx...->vzk.../dot_general | solution.py:37
  525.9 13.1 %fusion.407 = (f32[]{:T(128)}, f32[16,128,512]{2,1,0:T(8,128)}) fusion(f32[16,128,512]{2,1,0:T(8,128)S(1)} %fusion.121, f32[16,512,128]{1,2,0:T(8,128)S(1)} %copy-done.17), kind=kOutput, calls=%fused_computation.410 | convolution fusion | flops 6449266688 | bytes 12582916 | tf_op jit(solution)/shard_map/kx,vzx...->vzk.../dot_general | solution.py:37
  539.0 9.5 pmax.14
  557.7 9.5 all-reduce.3
  570.5 19.2 %fusion.13 = (f32[64,128,128]{2,0,1:T(8,128)}, f32[64,128,128]{2,0,1:T(8,128)}) fusion(f32[128,128,64]{1,2,0:T(8,128)} %convolution_subtract_fusion, f32[128,128,64]{1,2,0:T(8,128)} %convolution_add_fusion, f32[128]{0:T(128)S(1)} %broadcast_multiply_fusion.3, f32[64,128]{0,1:T(8,128)S(1)} %add_multiply_fusion.1), kind=kLoop, calls=%fused_computation.17 | loop fusion | flops 7340032 | bytes 16810496 | tf_op jit(solution)/shard_map/reduce_sum | solution.py:87
  589.7 175.1 %all-reduce.7.cloned.1.call-done = (f32[64,128,128]{2,0,1:T(8,128)}, f32[64,128,128]{2,0,1:T(8,128)}) async-done(((f32[64,128,128]{2,0,1:T(8,128)}, f32[64,128,128]{2,0,1:T(8,128)}), (f32[64,128,128]{2,0,1:T(8,128)}, f32[64,128,128]{2,0,1:T(8,128)})) %all-reduce.7.cloned.1.call-update) | async-done | bytes 8388624 | tf_op jit(solution)/shard_map/psum | solution.py:87
  764.8 10.4 fusion.24
  775.2 8.4 fusion.18
  783.7 6.3 fusion.16
  796.2 6.4 add_bitcast_fusion.3
  802.7 7.1 fusion.60
  809.8 8.2 add_bitcast_fusion.2
  823.2 8.8 fusion.62
  832.0 8.2 subtract_bitcast_fusion.2
  840.2 30.2 %all-to-all-done.5 = f32[1,64,128,128]{3,2,0,1:T(8,128)} async-done(((f32[1,64,128,128]{3,2,0,1:T(8,128)}), f32[1,64,128,128]{3,2,0,1:T(8,128)}, u32[]{:S(2)}, u32[]{:S(2)}) %all-to-all-start.5) | async-done | bytes 4194336 | tf_op jit(solution)/shard_map/all_to_all | solution.py:69
  886.0 36.3 %all-to-all-done.4 = f32[1,64,128,128]{3,2,0,1:T(8,128)} async-done(((f32[1,64,128,128]{3,2,0,1:T(8,128)}), f32[1,64,128,128]{3,2,0,1:T(8,128)}, u32[]{:S(2)}, u32[]{:S(2)}) %all-to-all-start.4) | async-done | bytes 4194336 | tf_op jit(solution)/shard_map/all_to_all | solution.py:68
  933.2 12.9 %fusion.119 = f32[16,128,512]{2,1,0:T(8,128)S(1)} fusion(f32[16,512,128]{1,2,0:T(8,128)} %reshape.469), kind=kOutput, calls=%fused_computation.133 | convolution fusion | flops 6446120960 | bytes 8388608 | tf_op jit(solution)/shard_map/kx,vzx...->vzk.../dot_general | solution.py:37
  946.1 13.1 %fusion.408 = (f32[]{:T(128)}, f32[16,128,512]{2,1,0:T(8,128)}) fusion(f32[16,128,512]{2,1,0:T(8,128)S(1)} %fusion.119, f32[16,512,128]{1,2,0:T(8,128)S(1)} %copy-done.18), kind=kOutput, calls=%fused_computation.411 | convolution fusion | flops 6449266688 | bytes 12582916 | tf_op jit(solution)/shard_map/kx,vzx...->vzk.../dot_general | solution.py:37
  959.2 9.5 pmax.15
  977.9 9.5 all-reduce.2
  990.8 21.9 %fusion.141 = f32[128,128,64]{1,2,0:T(8,128)S(1)} fusion(f32[128,128,64]{1,2,0:T(8,128)} %convolution_subtract_fusion, f32[128,128,64]{1,2,0:T(8,128)} %convolution_add_fusion, f32[128]{0:T(128)S(1)} %broadcast_multiply_fusion, f32[64,128]{0,1:T(8,128)S(1)} %add_multiply_fusion), kind=kOutput, calls=%fused_computation.144 | convolution fusion | flops 809558016 | bytes 12616192 | tf_op jit(solution)/shard_map/kz,vz...->vk.../dot_general | solution.py:33
  1012.8 19.8 %fusion.139 = f32[128,128,64]{1,2,0:T(8,128)S(1)} fusion(f32[128,128,64]{1,2,0:T(8,128)S(1)} %copy-done.1, f32[128,128,64]{1,2,0:T(8,128)S(1)} %copy-done, f32[128]{0:T(128)S(1)} %broadcast_multiply_fusion, f32[64,128]{0,1:T(8,128)S(1)} %add_multiply_fusion), kind=kOutput, calls=%fused_computation.143 | convolution fusion | flops 809558016 | bytes 12616192 | tf_op jit(solution)/shard_map/kz,vz...->vk.../dot_general | solution.py:33
  1032.6 19.6 %subtract_bitcast_fusion.1 = f32[64,128,128]{2,0,1:T(8,128)S(1)} fusion(f32[128,128,64]{1,2,0:T(8,128)S(1)} %fusion.141, f32[128,128,64]{1,2,0:T(8,128)S(1)} %copy-done.1, f32[128,128,64]{1,2,0:T(8,128)S(1)} %copy-done, f32[128]{0:T(128)S(1)} %broadcast_multiply_fusion, f32[64,128]{0,1:T(8,128)S(1)} %add_multiply_fusion), kind=kOutput, calls=%fused_computation.64 | convolution fusion | flops 810606592 | bytes 16810496 | tf_op jit(solution)/shard_map/kz,vz...->vk.../dot_general | solution.py:33
  1052.2 20.1 %add_bitcast_fusion.1 = f32[64,128,128]{2,0,1:T(8,128)S(1)} fusion(f32[128,128,64]{1,2,0:T(8,128)S(1)} %fusion.139, f32[128,128,64]{1,2,0:T(8,128)S(1)} %copy-done.1, f32[128,128,64]{1,2,0:T(8,128)S(1)} %copy-done, f32[128]{0:T(128)S(1)} %broadcast_multiply_fusion, f32[64,128]{0,1:T(8,128)S(1)} %add_multiply_fusion), kind=kOutput, calls=%fused_computation.63 | convolution fusion | flops 810606592 | bytes 16810496 | tf_op jit(solution)/shard_map/kz,vz...->vk.../dot_general | solution.py:33
  1072.4 7.0 fusion.52
  1079.4 8.2 add_bitcast_fusion
  1092.7 8.8 fusion.54
  1101.5 8.2 subtract_bitcast_fusion
  1109.7 25.1 %all-to-all-done.7 = f32[1,64,128,128]{3,2,0,1:T(8,128)} async-done(((f32[1,64,128,128]{3,2,0,1:T(8,128)}), f32[1,64,128,128]{3,2,0,1:T(8,128)}, u32[]{:S(2)}, u32[]{:S(2)}) %all-to-all-start.7) | async-done | bytes 4194336 | tf_op jit(solution)/shard_map/all_to_all | solution.py:69
  1150.4 36.2 %all-to-all-done.6 = f32[1,64,128,128]{3,2,0,1:T(8,128)} async-done(((f32[1,64,128,128]{3,2,0,1:T(8,128)}), f32[1,64,128,128]{3,2,0,1:T(8,128)}, u32[]{:S(2)}, u32[]{:S(2)}) %all-to-all-start.6) | async-done | bytes 4194336 | tf_op jit(solution)/shard_map/all_to_all | solution.py:68
  1197.5 12.9 %fusion.117 = f32[16,128,512]{2,1,0:T(8,128)S(1)} fusion(f32[16,512,128]{1,2,0:T(8,128)} %reshape.475), kind=kOutput, calls=%fused_computation.131 | convolution fusion | flops 6446120960 | bytes 8388608 | tf_op jit(solution)/shard_map/kx,vzx...->vzk.../dot_general | solution.py:37
  1210.5 12.5 %multiply_bitcast_fusion = f32[1,16,512,128]{2,3,1,0:T(8,128)} fusion(f32[16,128,512]{2,1,0:T(8,128)S(1)} %fusion.117, f32[16,512,128]{1,2,0:T(8,128)S(1)} %copy-done.15), kind=kOutput, calls=%fused_computation.60 | convolution fusion | flops 6448218112 | bytes 12582912 | tf_op jit(solution)/shard_map/kx,vzx...->vzk.../dot_general | solution.py:37
  (108 shorter events, 193.5 us)
Async XLA Ops:
  7.2 13.2 %copy-start.5 = (f32[1,16,512,128]{3,2,1,0:T(8,128)S(1)}, f32[1,16,512,128]{3,2,1,0:T(8,128)}, u32[]{:S(2)}) copy-start(f32[1,16,512,128]{3,2,1,0:T(8,128)} %param.1) | copy-start | bytes 12582916
  20.4 11.1 copy-start.4
  31.5 4.2 copy-start.2
  44.0 54.0 %all-to-all-start = ((f32[1,16,512,128]{3,1,0,2:T(8,128)}), f32[1,16,512,128]{3,1,0,2:T(8,128)}, u32[]{:S(2)}, u32[]{:S(2)}) async-start(f32[1,16,512,128]{3,1,0,2:T(8,128)} %copy.24), calls=%async_computation | async-start | bytes 8388608 | tf_op jit(solution)/shard_map/all_to_all | solution.py:51
  49.4 6.0 copy-start.3
  98.0 52.0 %all-to-all-start.1 = ((f32[1,16,512,128]{3,1,0,2:T(8,128)}), f32[1,16,512,128]{3,1,0,2:T(8,128)}, u32[]{:S(2)}, u32[]{:S(2)}) async-start(f32[1,16,512,128]{3,1,0,2:T(8,128)} %copy.26), calls=%async_computation.1 | async-start | bytes 8388608 | tf_op jit(solution)/shard_map/all_to_all | solution.py:52
  103.0 241.4 %all-reduce.9.cloned.1.call-start = ((), (), s32[]{:S(2)}) async-start(), calls=%async_computation.9 | async-start | bytes 16777216 | tf_op jit(solution)/shard_map/psum | solution.py:87
  106.0 2.0 copy-start.8
  152.9 4.2 copy-start.16
  157.0 5.4 copy-start.9
  354.8 8.4 copy-start.21
  375.8 13.5 %copy-start.11 = (f32[64,128,128]{2,0,1:T(8,128)}, f32[64,128,128]{2,0,1:T(8,128)S(1)}, u32[]{:S(2)}) copy-start(f32[64,128,128]{2,0,1:T(8,128)S(1)} %subtract_bitcast_fusion.5) | copy-start | bytes 12582916
  382.2 7.1 copy-start.19
  397.5 52.6 %all-to-all-start.3 = ((f32[1,64,128,128]{3,2,0,1:T(8,128)}), f32[1,64,128,128]{3,2,0,1:T(8,128)}, u32[]{:S(2)}, u32[]{:S(2)}) async-start(f32[1,64,128,128]{3,2,0,1:T(8,128)} %add_bitcast_fusion.4), calls=%async_computation.3 | async-start | bytes 8388608 | tf_op jit(solution)/shard_map/all_to_all | solution.py:69
  402.8 8.8 copy-start.12
  450.1 51.9 %all-to-all-start.2 = ((f32[1,64,128,128]{3,2,0,1:T(8,128)}), f32[1,64,128,128]{3,2,0,1:T(8,128)}, u32[]{:S(2)}, u32[]{:S(2)}) async-start(f32[1,64,128,128]{3,2,0,1:T(8,128)} %subtract_bitcast_fusion.4), calls=%async_computation.2 | async-start | bytes 8388608 | tf_op jit(solution)/shard_map/all_to_all | solution.py:68
  455.1 309.8 %all-reduce.7.cloned.1.call-start = ((), (), s32[]{:S(2)}) async-start(), calls=%async_computation.8 | async-start | bytes 16777216 | tf_op jit(solution)/shard_map/psum | solution.py:87
  512.9 13.0 %copy-start.17 = (f32[16,512,128]{1,2,0:T(8,128)S(1)}, f32[16,512,128]{1,2,0:T(8,128)}, u32[]{:S(2)}) copy-start(f32[16,512,128]{1,2,0:T(8,128)} %reshape.464) | copy-start | bytes 12582916
  775.2 8.4 copy-start.22
  796.2 13.5 %copy-start.13 = (f32[64,128,128]{2,0,1:T(8,128)}, f32[64,128,128]{2,0,1:T(8,128)S(1)}, u32[]{:S(2)}) copy-start(f32[64,128,128]{2,0,1:T(8,128)S(1)} %subtract_bitcast_fusion.3) | copy-start | bytes 12582916
  802.7 7.1 copy-start.20
  818.0 52.4 %all-to-all-start.5 = ((f32[1,64,128,128]{3,2,0,1:T(8,128)}), f32[1,64,128,128]{3,2,0,1:T(8,128)}, u32[]{:S(2)}, u32[]{:S(2)}) async-start(f32[1,64,128,128]{3,2,0,1:T(8,128)} %add_bitcast_fusion.2), calls=%async_computation.5 | async-start | bytes 8388608 | tf_op jit(solution)/shard_map/all_to_all | solution.py:69
  823.2 8.8 copy-start.14
  870.4 51.9 %all-to-all-start.4 = ((f32[1,64,128,128]{3,2,0,1:T(8,128)}), f32[1,64,128,128]{3,2,0,1:T(8,128)}, u32[]{:S(2)}, u32[]{:S(2)}) async-start(f32[1,64,128,128]{3,2,0,1:T(8,128)} %subtract_bitcast_fusion.2), calls=%async_computation.4 | async-start | bytes 8388608 | tf_op jit(solution)/shard_map/all_to_all | solution.py:68
  933.2 13.0 %copy-start.18 = (f32[16,512,128]{1,2,0:T(8,128)S(1)}, f32[16,512,128]{1,2,0:T(8,128)}, u32[]{:S(2)}) copy-start(f32[16,512,128]{1,2,0:T(8,128)} %reshape.470) | copy-start | bytes 12582916
  988.1 24.6 %copy-start.23 = (f32[1,3]{1,0:T(1,128)}, f32[1,3]{1,0:T(1,128)S(1)}, u32[]{:S(2)}) copy-start(f32[1,3]{1,0:T(1,128)S(1)} %broadcast_divide_fusion) | copy-start | bytes 40
  990.8 21.9 %copy-start = (f32[128,128,64]{1,2,0:T(8,128)S(1)}, f32[128,128,64]{1,2,0:T(8,128)}, u32[]{:S(2)}) copy-start(f32[128,128,64]{1,2,0:T(8,128)} %convolution_add_fusion) | copy-start | bytes 12582916
  990.8 21.9 %copy-start.1 = (f32[128,128,64]{1,2,0:T(8,128)S(1)}, f32[128,128,64]{1,2,0:T(8,128)}, u32[]{:S(2)}) copy-start(f32[128,128,64]{1,2,0:T(8,128)} %convolution_subtract_fusion) | copy-start | bytes 12582916
  1052.2 27.2 %copy-start.6 = (f32[64,128,128]{2,0,1:T(8,128)}, f32[64,128,128]{2,0,1:T(8,128)S(1)}, u32[]{:S(2)}) copy-start(f32[64,128,128]{2,0,1:T(8,128)S(1)} %subtract_bitcast_fusion.1) | copy-start | bytes 12582916
  1072.3 7.1 copy-start.10
  1087.6 47.1 %all-to-all-start.7 = ((f32[1,64,128,128]{3,2,0,1:T(8,128)}), f32[1,64,128,128]{3,2,0,1:T(8,128)}, u32[]{:S(2)}, u32[]{:S(2)}) async-start(f32[1,64,128,128]{3,2,0,1:T(8,128)} %add_bitcast_fusion), calls=%async_computation.7 | async-start | bytes 8388608 | tf_op jit(solution)/shard_map/all_to_all | solution.py:69
  1092.7 8.8 copy-start.7
  1134.8 51.8 %all-to-all-start.6 = ((f32[1,64,128,128]{3,2,0,1:T(8,128)}), f32[1,64,128,128]{3,2,0,1:T(8,128)}, u32[]{:S(2)}, u32[]{:S(2)}) async-start(f32[1,64,128,128]{3,2,0,1:T(8,128)} %subtract_bitcast_fusion), calls=%async_computation.6 | async-start | bytes 8388608 | tf_op jit(solution)/shard_map/all_to_all | solution.py:68
  1197.5 13.0 %copy-start.15 = (f32[16,512,128]{1,2,0:T(8,128)S(1)}, f32[16,512,128]{1,2,0:T(8,128)}, u32[]{:S(2)}) copy-start(f32[16,512,128]{1,2,0:T(8,128)} %reshape.476) | copy-start | bytes 12582916
Sparse Core Ops, SparseCore 0:
  168.4 175.9 all-reduce.8
  589.8 174.9 all-reduce.6
where the time goes:
time: 1250 us; the launch traced here: 1240 us
  waiting for transfers between devices  617 us (49%)
  matrix products  373 us (30%)
  local copies, waits for them, and re-layouts  87.9 us (7%)
  other arithmetic  59.8 us (5%)
  starting transfers between devices  40.9 us (3%)
  blocking collectives  38 us (3%)
  between operations  19.1 us (2%)
    psum x2, waiting for transfers between devices, template_sum(): lax.psum((jnp.sum(spectrum[0], axis=0), jnp.sum(spectrum[1], axis=0)), 'tm')  351 us
    dot_general x16, matrix products, mix_z(): return jnp.einsum('kz,vz...->vk...', table, data, precision=precise)  157 us
    dot_general x16, matrix products, mix_y(): return jnp.dot(data, table, precision=precise)  115 us
    all_to_all x3, waiting for transfers between devices, inverse(): lax.all_to_all(real_y, 'space', split_axis=1, concat_axis=2, tiled=True)  109 us
    dot_general x8, matrix products, mix_x(): return jnp.einsum('kx,vzx...->vzk...', table, data, precision=precise)  102 us
    all_to_all x3, waiting for transfers between devices, inverse(): lax.all_to_all(imag_y, 'space', split_axis=1, concat_axis=2, tiled=True)  85.7 us
    all_to_all x1, waiting for transfers between devices, forward(): lax.all_to_all(imag_y, 'space', split_axis=2, concat_axis=1, tiled=True)  36.6 us
    all_to_all x1, waiting for transfers between devices, forward(): lax.all_to_all(real_y, 'space', split_axis=2, concat_axis=1, tiled=True)  34.3 us
  transfers between devices with their start and end apart: 10, of which 10 were waited for; matrix products, arithmetic and copies ran while one was open for 9% of the time, Pallas kernels for 0%

commit v1 on v0

--- a/solution.py
+++ b/solution.py
@@ -11,6 +11,18 @@
 precise = lax.Precision.HIGHEST
 sharpness = 256.0
 floor_share = 0.05
+
+
+def sent_to_each(array, axis, split, join):
+    ways, here = (lax.axis_size(axis), lax.axis_index(axis))
+    width = array.shape[split] // ways
+    turned = jnp.roll(array, -here * width, axis=split)
+    got = [lax.slice_in_dim(turned, 0, width, axis=split)]
+    for far in range(1, ways):
+        sent = lax.slice_in_dim(turned, far * width, (far + 1) * width, axis=split)
+        got.append(lax.ppermute(sent, axis, [(d, (d + far) % ways) for d in range(ways)]))
+    line = jnp.concatenate(got[::-1], axis=join)
+    return jnp.roll(line, (here + 1) * got[0].shape[join], axis=join)
 
 
 def dft_tables(length):
@@ -66,7 +78,7 @@
     imag_y = mix_y(real_z, sin_y) + mix_y(imag_z, cos_y)
     real_s, imag_s = (
         lax.all_to_all(real_y, "space", split_axis=1, concat_axis=2, tiled=True),
-        lax.all_to_all(imag_y, "space", split_axis=1, concat_axis=2, tiled=True),
+        sent_to_each(imag_y, "space", 1, 2),
     )
     return (mix_x(cos_x, real_s) - mix_x(sin_x, imag_s)) * norming
 

time: 1250 us -> 1190 us (0.952)
  waiting for transfers between devices: 617 us -> 554 us
  matrix products: 373 us -> 403 us
  local copies, waits for them, and re-layouts: 87.9 us -> 59.7 us
    all_to_all x3 -> x0, waiting for transfers between devices: 85.7 us -> none  [inverse(): lax.all_to_all(imag_y, 'space', split_axis=1, concat_axis=2, tiled=True)]
    ppermute x0 -> x9, waiting for transfers between devices: none -> 53.5 us  [sent_to_each(): lax.ppermute(sent, axis, [(d, (d + far) % ways) for d in range(ways)])]
    dot_general x8, matrix products: 102 us -> 135 us  [mix_x(): return jnp.einsum('kx,vzx...->vzk...', table, data, precision=precise)]
    all_to_all x3, waiting for transfers between devices: 109 us -> 77.7 us  [inverse(): lax.all_to_all(real_y, 'space', split_axis=1, concat_axis=2, tiled=True)]
    another operation x6 -> x3, local copies, waits for them, and re-layouts: 33.2 us -> 17.1 us
    all_to_all x3 -> x0, local copies, waits for them, and re-layouts: 15.8 us -> none  [inverse(): lax.all_to_all(imag_y, 'space', split_axis=1, concat_axis=2, tiled=True)]
    all_to_all x3 -> x0, starting transfers between devices: 15.5 us -> none  [inverse(): lax.all_to_all(imag_y, 'space', split_axis=1, concat_axis=2, tiled=True)]
  transfers between devices with their start and end apart: 10 -> 16, of which waited for: 10 -> 10; matrix products, arithmetic and copies ran while one was open for 9% -> 13% of each run, Pallas kernels for 0% -> 0%
where the time goes in v1:
time: 1190 us; the launch traced here: 1180 us
  waiting for transfers between devices  554 us (47%)
  matrix products  403 us (34%)
  other arithmetic  64.8 us (5%)
  local copies, waits for them, and re-layouts  59.7 us (5%)
  blocking collectives  40.2 us (3%)
  starting transfers between devices  37.9 us (3%)
  between operations  19 us (2%)
    psum x2, waiting for transfers between devices, template_sum(): lax.psum((jnp.sum(spectrum[0], axis=0), jnp.sum(spectrum[1], axis=0)), 'tm')  352 us
    dot_general x16, matrix products, mix_z(): return jnp.einsum('kz,vz...->vk...', table, data, precision=precise)  157 us
    dot_general x8, matrix products, mix_x(): return jnp.einsum('kx,vzx...->vzk...', table, data, precision=precise)  135 us
    dot_general x16, matrix products, mix_y(): return jnp.dot(data, table, precision=precise)  111 us
    all_to_all x3, waiting for transfers between devices, inverse(): lax.all_to_all(real_y, 'space', split_axis=1, concat_axis=2, tiled=True)  77.7 us
    ppermute x9, waiting for transfers between devices, sent_to_each(): lax.ppermute(sent, axis, [(d, (d + far) % ways) for d in range(ways)])  53.5 us
    all_to_all x1, waiting for transfers between devices, forward(): lax.all_to_all(imag_y, 'space', split_axis=2, concat_axis=1, tiled=True)  36.6 us
    all_to_all x1, waiting for transfers between devices, forward(): lax.all_to_all(real_y, 'space', split_axis=2, concat_axis=1, tiled=True)  34.3 us
  transfers between devices with their start and end apart: 16, of which 10 were waited for; matrix products, arithmetic and copies ran while one was open for 13% of the time, Pallas kernels for 0%

profile of v1, /device:TPU:0, one launch (start us, length us, event | category | flops | bytes accessed | tf_op | source)
XLA Modules:
  0.0 1179.5 jit_solution(2725954101040737801)
XLA Ops:
  7.2 13.2 %fusion.82 = f32[512,16,128]{2,0,1:T(8,128)S(1)} fusion(f32[1,16,512,128]{3,2,1,0:T(8,128)} %param.5), kind=kOutput, calls=%fused_computation.118 | convolution fusion | flops 6446120960 | bytes 8388608 | tf_op jit(solution)/shard_map/kx,vzx...->vzk.../dot_general | solution.py:49
  20.4 11.1 fusion.80
  63.7 34.3 %all-to-all-done = f32[1,16,512,128]{3,1,0,2:T(8,128)} async-done(((f32[1,16,512,128]{3,1,0,2:T(8,128)}), f32[1,16,512,128]{3,1,0,2:T(8,128)}, u32[]{:S(2)}, u32[]{:S(2)}) %all-to-all-start) | async-done | bytes 4194336 | tf_op jit(solution)/shard_map/all_to_all | solution.py:63
  113.4 36.6 %all-to-all-done.1 = f32[1,16,512,128]{3,1,0,2:T(8,128)} async-done(((f32[1,16,512,128]{3,1,0,2:T(8,128)}), f32[1,16,512,128]{3,1,0,2:T(8,128)}, u32[]{:S(2)}, u32[]{:S(2)}) %all-to-all-start.1) | async-done | bytes 4194336 | tf_op jit(solution)/shard_map/all_to_all | solution.py:64
  168.3 176.1 %all-reduce.9.cloned.1.call-done = (f32[64,128,128]{2,0,1:T(8,128)}, f32[64,128,128]{2,0,1:T(8,128)}) async-done(((f32[64,128,128]{2,0,1:T(8,128)}, f32[64,128,128]{2,0,1:T(8,128)}), (f32[64,128,128]{2,0,1:T(8,128)}, f32[64,128,128]{2,0,1:T(8,128)})) %all-reduce.9.cloned.1.call-update) | async-done | bytes 8388624 | tf_op jit(solution)/shard_map/psum | solution.py:99
  344.4 10.4 fusion.70
  354.8 8.4 fusion.64
  363.2 6.3 fusion.62
  369.6 6.2 subtract_bitcast_fusion.5
  375.8 6.6 add_bitcast_fusion.5
  382.4 7.1 fusion.106
  389.5 8.2 subtract_bitcast_fusion.4
  402.9 8.7 fusion.104
  411.6 7.1 add_bitcast_fusion.4
  425.7 25.9 %all-to-all-done.2 = f32[1,64,128,128]{3,2,0,1:T(8,128)} async-done(((f32[1,64,128,128]{3,2,0,1:T(8,128)}), f32[1,64,128,128]{3,2,0,1:T(8,128)}, u32[]{:S(2)}, u32[]{:S(2)}) %all-to-all-start.2) | async-done | bytes 4194336 | tf_op jit(solution)/shard_map/all_to_all | solution.py:80
  462.6 13.4 %fusion.163 = f32[16,128,512]{2,1,0:T(8,128)S(1)} fusion(f32[16,512,128]{1,2,0:T(8,128)} %reshape.460), kind=kOutput, calls=%fused_computation.195 | convolution fusion | flops 6446120960 | bytes 8388608 | tf_op jit(solution)/shard_map/kx,vzx...->vzk.../dot_general | solution.py:49
  476.1 19.9 %collective-permute-done.2 = f32[1,16,128,128]{3,2,1,0:T(8,128)} collective-permute-done((f32[1,16,128,128]{3,2,1,0:T(8,128)S(1)}, f32[1,16,128,128]{3,2,1,0:T(8,128)}, u32[]{:S(2)}, u32[]{:S(2)}) %collective-permute-start.2) | collective-permute-done | bytes 1048608 | tf_op jit(solution)/shard_map/ppermute | solution.py:23
  496.0 23.5 %fusion.455 = (f32[]{:T(128)}, f32[16,128,512]{2,1,0:T(8,128)}) fusion(f32[16,128,512]{2,1,0:T(8,128)S(1)} %fusion.163, s32[]{:T(128)S(6)} %select_n.238, f32[1,16,128,128]{3,2,1,0:T(8,128)} %collective-permute-done, f32[1,16,128,128]{3,2,1,0:T(8,128)} %collective-permute-done.1, f32[1,16,128,128]{3,2,1,0:T(8,128)} %collective-permute-done.2, ...), kind=kOutput, calls=%fused_computation.476 | convolution fusion | flops 6456606720 | bytes 12582920 | tf_op jit(solution)/shard_map/kx,vzx...->vzk.../dot_general | solution.py:49
  519.5 12.1 %pmax.14 = f32[]{:T(128)} all-reduce(f32[]{:T(128)} %get-tuple-element.50), channel_id=1, replica_groups=mesh['tm'=8,'space'=4] {'space'}, use_global_device_ids=true, to_apply=%region_3.6 | all-reduce | flops 1 | bytes 8 | tf_op jit(solution)/shard_map/pmax | solution.py:113
  540.8 8.1 all-reduce.3
  552.2 19.2 %fusion.13 = (f32[64,128,128]{2,0,1:T(8,128)}, f32[64,128,128]{2,0,1:T(8,128)}) fusion(f32[128,128,64]{1,2,0:T(8,128)} %convolution_subtract_fusion, f32[128,128,64]{1,2,0:T(8,128)} %convolution_add_fusion, f32[128]{0:T(128)S(1)} %broadcast_multiply_fusion.3, f32[64,128]{0,1:T(8,128)S(1)} %add_multiply_fusion.1), kind=kLoop, calls=%fused_computation.47 | loop fusion | flops 7340032 | bytes 16810496 | tf_op jit(solution)/shard_map/reduce_sum | solution.py:99
  571.4 176.3 %all-reduce.7.cloned.1.call-done = (f32[64,128,128]{2,0,1:T(8,128)}, f32[64,128,128]{2,0,1:T(8,128)}) async-done(((f32[64,128,128]{2,0,1:T(8,128)}, f32[64,128,128]{2,0,1:T(8,128)}), (f32[64,128,128]{2,0,1:T(8,128)}, f32[64,128,128]{2,0,1:T(8,128)})) %all-reduce.7.cloned.1.call-update) | async-done | bytes 8388624 | tf_op jit(solution)/shard_map/psum | solution.py:99
  747.7 10.4 fusion.60
  758.1 8.4 fusion.54
  766.5 6.3 fusion.52
  779.1 6.6 add_bitcast_fusion.3
  785.7 7.1 fusion.98
  792.8 8.2 subtract_bitcast_fusion.2
  805.9 8.9 fusion.96
  814.8 7.1 add_bitcast_fusion.2
  828.9 25.8 %all-to-all-done.3 = f32[1,64,128,128]{3,2,0,1:T(8,128)} async-done(((f32[1,64,128,128]{3,2,0,1:T(8,128)}), f32[1,64,128,128]{3,2,0,1:T(8,128)}, u32[]{:S(2)}, u32[]{:S(2)}) %all-to-all-start.3) | async-done | bytes 4194336 | tf_op jit(solution)/shard_map/all_to_all | solution.py:80
  865.6 13.4 %fusion.161 = f32[16,128,512]{2,1,0:T(8,128)S(1)} fusion(f32[16,512,128]{1,2,0:T(8,128)} %reshape.466), kind=kOutput, calls=%fused_computation.193 | convolution fusion | flops 6446120960 | bytes 8388608 | tf_op jit(solution)/shard_map/kx,vzx...->vzk.../dot_general | solution.py:49
  879.0 20.1 %collective-permute-done.5 = f32[1,16,128,128]{3,2,1,0:T(8,128)} collective-permute-done((f32[1,16,128,128]{3,2,1,0:T(8,128)S(1)}, f32[1,16,128,128]{3,2,1,0:T(8,128)}, u32[]{:S(2)}, u32[]{:S(2)}) %collective-permute-start.5) | collective-permute-done | bytes 1048608 | tf_op jit(solution)/shard_map/ppermute | solution.py:23
  899.1 23.8 %fusion.456 = (f32[]{:T(128)}, f32[16,128,512]{2,1,0:T(8,128)}) fusion(f32[16,128,512]{2,1,0:T(8,128)S(1)} %fusion.161, s32[]{:T(128)S(6)} %select_n.238, f32[1,16,128,128]{3,2,1,0:T(8,128)} %collective-permute-done.3, f32[1,16,128,128]{3,2,1,0:T(8,128)} %collective-permute-done.4, f32[1,16,128,128]{3,2,1,0:T(8,128)} %collective-permute-done.5, ...), kind=kOutput, calls=%fused_computation.477 | convolution fusion | flops 6456606720 | bytes 12582920 | tf_op jit(solution)/shard_map/kx,vzx...->vzk.../dot_general | solution.py:49
  922.9 11.9 %pmax.15 = f32[]{:T(128)} all-reduce(f32[]{:T(128)} %get-tuple-element.52), channel_id=1, replica_groups=mesh['tm'=8,'space'=4] {'space'}, use_global_device_ids=true, to_apply=%region_16.19 | all-reduce | flops 1 | bytes 8 | tf_op jit(solution)/shard_map/pmax | solution.py:113
  944.0 8.1 all-reduce.2
  955.4 21.9 %fusion.183 = f32[128,128,64]{1,2,0:T(8,128)S(1)} fusion(f32[128,128,64]{1,2,0:T(8,128)} %convolution_subtract_fusion, f32[128,128,64]{1,2,0:T(8,128)} %convolution_add_fusion, f32[128]{0:T(128)S(1)} %get-tuple-element.54, f32[64,128]{0,1:T(8,128)S(1)} %add_multiply_fusion), kind=kOutput, calls=%fused_computation.204 | convolution fusion | flops 809558016 | bytes 12616192 | tf_op jit(solution)/shard_map/kz,vz...->vk.../dot_general | solution.py:45
  977.4 19.6 %fusion.181 = f32[128,128,64]{1,2,0:T(8,128)S(1)} fusion(f32[128,128,64]{1,2,0:T(8,128)S(1)} %copy-done.1, f32[128,128,64]{1,2,0:T(8,128)S(1)} %copy-done, f32[128]{0:T(128)S(1)} %get-tuple-element.54, f32[64,128]{0,1:T(8,128)S(1)} %add_multiply_fusion), kind=kOutput, calls=%fused_computation.203 | convolution fusion | flops 809558016 | bytes 12616192 | tf_op jit(solution)/shard_map/kz,vz...->vk.../dot_general | solution.py:45
  997.0 19.9 %subtract_bitcast_fusion.1 = f32[64,128,128]{2,0,1:T(8,128)S(1)} fusion(f32[128,128,64]{1,2,0:T(8,128)S(1)} %fusion.183, f32[128,128,64]{1,2,0:T(8,128)S(1)} %copy-done.1, f32[128,128,64]{1,2,0:T(8,128)S(1)} %copy-done, f32[128]{0:T(128)S(1)} %get-tuple-element.54, f32[64,128]{0,1:T(8,128)S(1)} %add_multiply_fusion), kind=kOutput, calls=%fused_computation.124 | convolution fusion | flops 810606592 | bytes 16810496 | tf_op jit(solution)/shard_map/kz,vz...->vk.../dot_general | solution.py:45
  1016.9 19.9 %add_bitcast_fusion.1 = f32[64,128,128]{2,0,1:T(8,128)S(1)} fusion(f32[128,128,64]{1,2,0:T(8,128)S(1)} %fusion.181, f32[128,128,64]{1,2,0:T(8,128)S(1)} %copy-done.1, f32[128,128,64]{1,2,0:T(8,128)S(1)} %copy-done, f32[128]{0:T(128)S(1)} %get-tuple-element.54, f32[64,128]{0,1:T(8,128)S(1)} %add_multiply_fusion), kind=kOutput, calls=%fused_computation.123 | convolution fusion | flops 810606592 | bytes 16810496 | tf_op jit(solution)/shard_map/kz,vz...->vk.../dot_general | solution.py:45
  1036.8 7.1 fusion.90
  1043.9 8.2 subtract_bitcast_fusion
  1057.4 8.7 fusion.88
  1066.1 7.1 add_bitcast_fusion
  1080.2 26.0 %all-to-all-done.4 = f32[1,64,128,128]{3,2,0,1:T(8,128)} async-done(((f32[1,64,128,128]{3,2,0,1:T(8,128)}), f32[1,64,128,128]{3,2,0,1:T(8,128)}, u32[]{:S(2)}, u32[]{:S(2)}) %all-to-all-start.4) | async-done | bytes 4194336 | tf_op jit(solution)/shard_map/all_to_all | solution.py:80
  1117.0 13.4 %fusion.159 = f32[16,128,512]{2,1,0:T(8,128)S(1)} fusion(f32[16,512,128]{1,2,0:T(8,128)} %reshape.472), kind=kOutput, calls=%fused_computation.191 | convolution fusion | flops 6446120960 | bytes 8388608 | tf_op jit(solution)/shard_map/kx,vzx...->vzk.../dot_general | solution.py:49
  1130.5 13.5 %collective-permute-done.8 = f32[1,16,128,128]{3,2,1,0:T(8,128)} collective-permute-done((f32[1,16,128,128]{3,2,1,0:T(8,128)S(1)}, f32[1,16,128,128]{3,2,1,0:T(8,128)}, u32[]{:S(2)}, u32[]{:S(2)}) %collective-permute-start.8) | collective-permute-done | bytes 1048608 | tf_op jit(solution)/shard_map/ppermute | solution.py:23
  1143.9 23.0 %multiply_bitcast_fusion = f32[1,16,512,128]{2,3,1,0:T(8,128)} fusion(f32[16,128,512]{2,1,0:T(8,128)S(1)} %fusion.159, s32[]{:T(128)S(6)} %select_n.238, f32[1,16,128,128]{3,2,1,0:T(8,128)} %collective-permute-done.6, f32[1,16,128,128]{3,2,1,0:T(8,128)} %collective-permute-done.7, f32[1,16,128,128]{3,2,1,0:T(8,128)} %collective-permute-done.8, ...), kind=kOutput, calls=%fused_computation.120 | convolution fusion | flops 6455558144 | bytes 12582916 | tf_op jit(solution)/shard_map/kx,vzx...->vzk.../dot_general | solution.py:49
  (113 shorter events, 167.4 us)
Async XLA Ops:
  7.2 13.2 %copy-start.5 = (f32[1,16,512,128]{3,2,1,0:T(8,128)S(1)}, f32[1,16,512,128]{3,2,1,0:T(8,128)}, u32[]{:S(2)}) copy-start(f32[1,16,512,128]{3,2,1,0:T(8,128)} %param.5) | copy-start | bytes 12582916
  20.4 11.1 copy-start.4
  31.5 4.2 copy-start.2
  44.0 54.0 %all-to-all-start = ((f32[1,16,512,128]{3,1,0,2:T(8,128)}), f32[1,16,512,128]{3,1,0,2:T(8,128)}, u32[]{:S(2)}, u32[]{:S(2)}) async-start(f32[1,16,512,128]{3,1,0,2:T(8,128)} %copy.42), calls=%async_computation | async-start | bytes 8388608 | tf_op jit(solution)/shard_map/all_to_all | solution.py:63
  49.4 6.0 copy-start.3
  98.0 52.0 %all-to-all-start.1 = ((f32[1,16,512,128]{3,1,0,2:T(8,128)}), f32[1,16,512,128]{3,1,0,2:T(8,128)}, u32[]{:S(2)}, u32[]{:S(2)}) async-start(f32[1,16,512,128]{3,1,0,2:T(8,128)} %copy.44), calls=%async_computation.1 | async-start | bytes 8388608 | tf_op jit(solution)/shard_map/all_to_all | solution.py:64
  103.0 241.4 %all-reduce.9.cloned.1.call-start = ((), (), s32[]{:S(2)}) async-start(), calls=%async_computation.6 | async-start | bytes 16777216 | tf_op jit(solution)/shard_map/psum | solution.py:99
  106.0 2.0 copy-start.8
  152.9 4.2 copy-start.15
  157.0 5.4 copy-start.9
  354.8 8.4 copy-start.18
  375.8 13.7 %copy-start.11 = (f32[64,128,128]{2,0,1:T(8,128)}, f32[64,128,128]{2,0,1:T(8,128)S(1)}, u32[]{:S(2)}) copy-start(f32[64,128,128]{2,0,1:T(8,128)S(1)} %subtract_bitcast_fusion.5) | copy-start | bytes 12582916
  382.4 7.1 copy-start.16
  397.8 53.8 %all-to-all-start.2 = ((f32[1,64,128,128]{3,2,0,1:T(8,128)}), f32[1,64,128,128]{3,2,0,1:T(8,128)}, u32[]{:S(2)}, u32[]{:S(2)}) async-start(f32[1,64,128,128]{3,2,0,1:T(8,128)} %subtract_bitcast_fusion.4), calls=%async_computation.2 | async-start | bytes 8388608 | tf_op jit(solution)/shard_map/all_to_all | solution.py:80
  402.8 344.9 %all-reduce.7.cloned.1.call-start = ((), (), s32[]{:S(2)}) async-start(), calls=%async_computation.5 | async-start | bytes 16777216 | tf_op jit(solution)/shard_map/psum | solution.py:99
  402.9 8.7 copy-start.12
  421.6 54.4 %collective-permute-start = (f32[1,16,128,128]{3,2,1,0:T(8,128)}, f32[1,16,128,128]{3,2,1,0:T(8,128)}, u32[]{:S(2)}, u32[]{:S(2)}) collective-permute-start(f32[1,16,128,128]{3,2,1,0:T(8,128)} %get-tuple-element.43), channel_id=1, source_target_pairs={{0,3},{1,0},{2,1},{3,2},{4,7},{5,4},{6,5},{7,6},{8,11},{9,8},{10,9... | collective-permute-start | bytes 3145736 | tf_op jit(solution)/shard_map/ppermute | solution.py:23
  424.5 51.5 %collective-permute-start.1 = (f32[1,16,128,128]{3,2,1,0:T(8,128)S(1)}, f32[1,16,128,128]{3,2,1,0:T(8,128)}, u32[]{:S(2)}, u32[]{:S(2)}) collective-permute-start(f32[1,16,128,128]{3,2,1,0:T(8,128)S(1)} %get-tuple-element.42), channel_id=1, source_target_pairs={{0,2},{1,3},{2,0},{3,1},{4,6},{5,7},{6,4},{7,5},{8,10},{9,11},{10,... | collective-permute-start | bytes 3145736 | tf_op jit(solution)/shard_map/ppermute | solution.py:23
  425.1 70.9 %collective-permute-start.2 = (f32[1,16,128,128]{3,2,1,0:T(8,128)S(1)}, f32[1,16,128,128]{3,2,1,0:T(8,128)}, u32[]{:S(2)}, u32[]{:S(2)}) collective-permute-start(f32[1,16,128,128]{3,2,1,0:T(8,128)S(1)} %get-tuple-element.41), channel_id=1, source_target_pairs={{0,1},{1,2},{2,3},{3,0},{4,5},{5,6},{6,7},{7,4},{8,9},{9,10},{10,1... | collective-permute-start | bytes 3145736 | tf_op jit(solution)/shard_map/ppermute | solution.py:23
  758.1 8.4 copy-start.19
  779.1 13.7 %copy-start.13 = (f32[64,128,128]{2,0,1:T(8,128)}, f32[64,128,128]{2,0,1:T(8,128)S(1)}, u32[]{:S(2)}) copy-start(f32[64,128,128]{2,0,1:T(8,128)S(1)} %subtract_bitcast_fusion.3) | copy-start | bytes 12582916
  785.7 7.1 copy-start.17
  801.1 53.6 %all-to-all-start.3 = ((f32[1,64,128,128]{3,2,0,1:T(8,128)}), f32[1,64,128,128]{3,2,0,1:T(8,128)}, u32[]{:S(2)}, u32[]{:S(2)}) async-start(f32[1,64,128,128]{3,2,0,1:T(8,128)} %subtract_bitcast_fusion.2), calls=%async_computation.3 | async-start | bytes 8388608 | tf_op jit(solution)/shard_map/all_to_all | solution.py:80
  805.9 8.9 copy-start.14
  824.9 54.1 %collective-permute-start.3 = (f32[1,16,128,128]{3,2,1,0:T(8,128)}, f32[1,16,128,128]{3,2,1,0:T(8,128)}, u32[]{:S(2)}, u32[]{:S(2)}) collective-permute-start(f32[1,16,128,128]{3,2,1,0:T(8,128)} %get-tuple-element.39), channel_id=1, source_target_pairs={{0,3},{1,0},{2,1},{3,2},{4,7},{5,4},{6,5},{7,6},{8,11},{9,8},{10,9... | collective-permute-start | bytes 3145736 | tf_op jit(solution)/shard_map/ppermute | solution.py:23
  827.7 51.3 %collective-permute-start.4 = (f32[1,16,128,128]{3,2,1,0:T(8,128)S(1)}, f32[1,16,128,128]{3,2,1,0:T(8,128)}, u32[]{:S(2)}, u32[]{:S(2)}) collective-permute-start(f32[1,16,128,128]{3,2,1,0:T(8,128)S(1)} %get-tuple-element.38), channel_id=1, source_target_pairs={{0,2},{1,3},{2,0},{3,1},{4,6},{5,7},{6,4},{7,5},{8,10},{9,11},{10,... | collective-permute-start | bytes 3145736 | tf_op jit(solution)/shard_map/ppermute | solution.py:23
  828.3 70.8 %collective-permute-start.5 = (f32[1,16,128,128]{3,2,1,0:T(8,128)S(1)}, f32[1,16,128,128]{3,2,1,0:T(8,128)}, u32[]{:S(2)}, u32[]{:S(2)}) collective-permute-start(f32[1,16,128,128]{3,2,1,0:T(8,128)S(1)} %get-tuple-element.37), channel_id=1, source_target_pairs={{0,1},{1,2},{2,3},{3,0},{4,5},{5,6},{6,7},{7,4},{8,9},{9,10},{10,1... | collective-permute-start | bytes 3145736 | tf_op jit(solution)/shard_map/ppermute | solution.py:23
  952.7 24.6 %copy-start.20 = (f32[1,3]{1,0:T(1,128)}, f32[1,3]{1,0:T(1,128)S(1)}, u32[]{:S(2)}) copy-start(f32[1,3]{1,0:T(1,128)S(1)} %broadcast_divide_fusion) | copy-start | bytes 40
  955.4 22.0 %copy-start = (f32[128,128,64]{1,2,0:T(8,128)S(1)}, f32[128,128,64]{1,2,0:T(8,128)}, u32[]{:S(2)}) copy-start(f32[128,128,64]{1,2,0:T(8,128)} %convolution_add_fusion) | copy-start | bytes 12582916
  955.4 22.0 %copy-start.1 = (f32[128,128,64]{1,2,0:T(8,128)S(1)}, f32[128,128,64]{1,2,0:T(8,128)}, u32[]{:S(2)}) copy-start(f32[128,128,64]{1,2,0:T(8,128)} %convolution_subtract_fusion) | copy-start | bytes 12582916
  1016.9 27.0 %copy-start.6 = (f32[64,128,128]{2,0,1:T(8,128)}, f32[64,128,128]{2,0,1:T(8,128)S(1)}, u32[]{:S(2)}) copy-start(f32[64,128,128]{2,0,1:T(8,128)S(1)} %subtract_bitcast_fusion.1) | copy-start | bytes 12582916
  1036.8 7.1 copy-start.10
  1052.1 54.1 %all-to-all-start.4 = ((f32[1,64,128,128]{3,2,0,1:T(8,128)}), f32[1,64,128,128]{3,2,0,1:T(8,128)}, u32[]{:S(2)}, u32[]{:S(2)}) async-start(f32[1,64,128,128]{3,2,0,1:T(8,128)} %subtract_bitcast_fusion), calls=%async_computation.4 | async-start | bytes 8388608 | tf_op jit(solution)/shard_map/all_to_all | solution.py:80
  1057.4 8.7 copy-start.7
  1076.2 54.3 %collective-permute-start.6 = (f32[1,16,128,128]{3,2,1,0:T(8,128)}, f32[1,16,128,128]{3,2,1,0:T(8,128)}, u32[]{:S(2)}, u32[]{:S(2)}) collective-permute-start(f32[1,16,128,128]{3,2,1,0:T(8,128)} %get-tuple-element.35), channel_id=1, source_target_pairs={{0,3},{1,0},{2,1},{3,2},{4,7},{5,4},{6,5},{7,6},{8,11},{9,8},{10,9... | collective-permute-start | bytes 3145736 | tf_op jit(solution)/shard_map/ppermute | solution.py:23
  1079.1 51.4 %collective-permute-start.7 = (f32[1,16,128,128]{3,2,1,0:T(8,128)S(1)}, f32[1,16,128,128]{3,2,1,0:T(8,128)}, u32[]{:S(2)}, u32[]{:S(2)}) collective-permute-start(f32[1,16,128,128]{3,2,1,0:T(8,128)S(1)} %get-tuple-element.34), channel_id=1, source_target_pairs={{0,2},{1,3},{2,0},{3,1},{4,6},{5,7},{6,4},{7,5},{8,10},{9,11},{10,... | collective-permute-start | bytes 3145736 | tf_op jit(solution)/shard_map/ppermute | solution.py:23
  1079.7 64.3 %collective-permute-start.8 = (f32[1,16,128,128]{3,2,1,0:T(8,128)S(1)}, f32[1,16,128,128]{3,2,1,0:T(8,128)}, u32[]{:S(2)}, u32[]{:S(2)}) collective-permute-start(f32[1,16,128,128]{3,2,1,0:T(8,128)S(1)} %get-tuple-element.33), channel_id=1, source_target_pairs={{0,1},{1,2},{2,3},{3,0},{4,5},{5,6},{6,7},{7,4},{8,9},{9,10},{10,1... | collective-permute-start | bytes 3145736 | tf_op jit(solution)/shard_map/ppermute | solution.py:23
Sparse Core Ops, SparseCore 0:
  168.4 175.9 all-reduce.8
  571.5 176.1 all-reduce.6
